TPU v7x, 32 devices: a whole 2x2x4 slice. The times are simulated.
32 devices in a mesh: rec: 2 (over y), gx: 16 (over z, x, core).
Axes of the slice: x: 2, y: 2, z: 4, core: 2. Of those that a mesh axis runs over, the one named last changes fastest.
Arguments:
- velocity: float32 [4, 3, 96, 16, 128], P(None, None, ('rec', 'gx')), parts along dimension 2, may hold values from -6 to 36, as said below
- span_rim: float32 [4, 2, 96, 10, 6], P(None, None, ('rec', 'gx')), parts along dimension 2, may hold values from -6 to 36, as said below
- sketch_old: bfloat16 [3, 96, 10, 128, 256], P(None, ('rec', 'gx')), parts along dimension 1, as said below
- omega: float32 [4, 256], replicated, may hold values from -6 to 6
Outputs:
- basis: bfloat16 [3, 96, 10, 128, 256], P(None, ('rec', 'gx')), parts along dimension 1
- factor: float32 [512, 256], P('rec'), parts along dimension 0
There are 2 independent parts, one for each index of `rec`. A program takes and returns all parts, laid end to end along the dimension named above; an argument that names none is the same for every part. Nothing has to cross between parts.
Inputs may be any that keep to these rules, and one draw needn't show every extreme that they name: `sketch_old`: finite values of order one; rows differ in scale. `velocity`: finite values. `span_rim`: finite values.
All inputs are finite; a program needn't handle non-finite values.
Results may differ from a plain program's by a relative error of at most 0.014.
The roundings to bfloat16 on the way count: a program that leaves them out, or rounds other values in their place, can miss the bound.
Values sent between devices are 32-bit elements; how exact they have to be, the bound alone decides.
No kernel may reach another device: no remote copies, remote signals or barrier semaphores. Data moves between devices by JAX's collectives and lax.ppermute only.
A program may use at most 64 MiB of HBM per device.

v0:
```python
import jax
import jax.numpy as jnp
from jax import lax
from jax.sharding import PartitionSpec as P

COEFS = (0.75, -0.15, 1.0 / 60.0)


def extended_2(cells, sides, width):
    for axis, dim in sides:
        count = lax.axis_size(axis)
        head = lax.slice_in_dim(cells, 0, width, axis=dim)
        tail = lax.slice_in_dim(cells, cells.shape[dim] - width, cells.shape[dim], axis=dim)
        cells = jnp.concatenate(
            [
                lax.ppermute(tail, axis, [(i, (i + 1) % count) for i in range(count)]),
                cells,
                lax.ppermute(head, axis, [((i + 1) % count, i) for i in range(count)]),
            ],
            axis=dim,
        )
    return cells


def band_diff(padded, axis, count):
    out_shape = list(padded.shape)
    out_shape[axis] = count
    total = jnp.zeros(tuple(out_shape), jnp.float32)
    for shift_k, weight in zip((1, 2, 3), COEFS):
        ahead = lax.slice_in_dim(padded, 3 + shift_k, 3 + shift_k + count, axis=axis)
        behind = lax.slice_in_dim(padded, 3 - shift_k, 3 - shift_k + count, axis=axis)
        total = total + weight * (ahead - behind)
    return total


def span_extend(field, rim_part):
    return jnp.concatenate([rim_part[..., :3], field, rim_part[..., 3:]], axis=-1)


def upper_factor(gram):
    order = gram.shape[0]
    index = jnp.arange(order, dtype=jnp.int32)

    def column_step(j, lower):
        pick = (index == j).astype(gram.dtype)
        row = jnp.dot(pick, lower, precision=lax.Precision.HIGHEST)
        column = jnp.dot(gram, pick, precision=lax.Precision.HIGHEST) - jnp.dot(
            lower, row, precision=lax.Precision.HIGHEST
        )
        pivot = jnp.sqrt(jnp.sum(column * pick))
        below = (index > j).astype(gram.dtype)
        fresh = column * below / pivot + pick * pivot
        return lower + fresh[:, None] * pick[None, :]

    lower = lax.fori_loop(0, order, column_step, jnp.zeros_like(gram))
    return lower.T


def inverse_upper(upper):
    order = upper.shape[0]
    index = jnp.arange(order, dtype=jnp.int32)
    lower = upper.T

    def row_step(j, solved):
        pick = (index == j).astype(upper.dtype)
        row = jnp.dot(pick, lower, precision=lax.Precision.HIGHEST)
        pivot = jnp.sum(row * pick)
        fresh = (pick - jnp.dot(row, solved, precision=lax.Precision.HIGHEST)) / pivot
        return solved + pick[:, None] * fresh[None, :]

    solved = lax.fori_loop(0, order, row_step, jnp.zeros_like(upper))
    return solved.T


def gram_of(matrix):
    return lax.dot_general(
        matrix, matrix, (((0,), (0,)), ((), ())), preferred_element_type=jnp.float32
    )


def local(velocity, span_rim, sketch_old, omega):
    slabs = velocity.shape[2]
    band_rows = velocity.shape[3] - 6
    span_cells = velocity.shape[4]
    extended = extended_2(velocity, (("gx", 2),), 3)
    v_ext = extended[:, 1, :, 3 : 3 + band_rows]
    w_ext = extended[:, 2, :, 3 : 3 + band_rows]
    band = velocity[:, :, :, 3 : 3 + band_rows]
    u_span = span_extend(band[:, 0], span_rim[:, 0])
    v_span = span_extend(band[:, 1], span_rim[:, 1])
    vort_x = band_diff(velocity[:, 2], 2, band_rows) - band_diff(v_span, 3, span_cells)
    vort_y = band_diff(u_span, 3, span_cells) - band_diff(w_ext, 1, slabs)
    vort_z = band_diff(v_ext, 1, slabs) - band_diff(velocity[:, 0], 2, band_rows)
    vort = jnp.stack([vort_x, vort_y, vort_z], axis=1)
    sketch = sketch_old.astype(jnp.float32)
    for snap in range(vort.shape[0]):
        sketch = sketch + vort[snap][..., None] * omega[snap]
    sketch = sketch.astype(jnp.bfloat16)
    matrix = sketch.reshape(-1, sketch.shape[-1])
    total = jnp.float32(matrix.shape[0] * lax.axis_size("gx"))
    local_gram = gram_of(matrix) / total
    factor = upper_factor(lax.psum(local_gram, "gx"))
    inverse_one = inverse_upper(factor).astype(jnp.bfloat16)
    basis = jnp.dot(matrix, inverse_one, preferred_element_type=jnp.float32).astype(jnp.bfloat16)
    return (basis.reshape(sketch.shape), factor)


def solution(mesh):
    in_specs = (
        P(None, None, ("rec", "gx"), None, None),
        P(None, None, ("rec", "gx"), None, None),
        P(None, ("rec", "gx"), None, None, None),
        P(),
    )
    out_specs = (P(None, ("rec", "gx"), None, None, None), P("rec", None))
    return jax.shard_map(local, mesh=mesh, in_specs=in_specs, out_specs=out_specs, check_vma=False)
```

profile of v0, /device:TPU:1, one launch (start us, length us, event | category | flops | bytes accessed | tf_op | source)
XLA Modules:
  0.0 1443.7 jit_solution(5448559899833227195)
XLA Ops:
  7.3 2.6 collective-permute-start
  14.8 2.3 collective-permute-done
  18.7 7.5 add_convert_fusion
  26.3 2.5 copy-done
  28.8 2.4 fusion.21
  31.3 91.8 %all-reduce.2.cloned.1.call-done = f32[256,256]{1,0:T(8,128)} async-done(((f32[256,256]{1,0:T(8,128)}), f32[256,256]{1,0:T(8,128)}) %all-reduce.2.cloned.1.call-update) | async-done | bytes 262160 | tf_op jit(solution)/shard_map/psum | solution.py:102
  123.1 829.0 %while.30 = (s32[]{:T(128)}, f32[256,256]{1,0:T(8,128)S(1)}, f32[256,256]{1,0:T(8,128)}, s32[]{:T(128)}, s32[]{:T(128)}) while((s32[]{:T(128)}, f32[256,256]{1,0:T(8,128)S(1)}, f32[256,256]{1,0:T(8,128)}, s32[]{:T(128)}, s32[]{:T(128)}) %tuple.85), condition=%wide.region_3.0_spmd.clone.clone, body=%wide.region_1.0_spmd.clone.clone.sunk | while | flops 2690306 | bytes 1324397 | solution.py:55
  126.5 1.2 fusion.114
  142.7 1.2 fusion.114
  146.0 1.2 fusion.114
  149.2 1.2 fusion.114
  152.4 1.2 fusion.114
  155.7 1.2 fusion.114
  158.9 1.2 fusion.114
  162.1 1.2 fusion.114
  165.4 1.2 fusion.114
  168.6 1.2 fusion.114
  171.9 1.2 fusion.114
  175.1 1.2 fusion.114
  178.3 1.2 fusion.114
  181.6 1.2 fusion.114
  184.8 1.2 fusion.114
  188.1 1.2 fusion.114
  204.2 1.2 fusion.114
  207.5 1.2 fusion.114
  210.7 1.2 fusion.114
  214.0 1.2 fusion.114
  217.2 1.2 fusion.114
  220.4 1.2 fusion.114
  223.7 1.2 fusion.114
  226.9 1.2 fusion.114
  230.1 1.2 fusion.114
  233.4 1.2 fusion.114
  236.6 1.2 fusion.114
  239.9 1.2 fusion.114
  243.1 1.2 fusion.114
  246.3 1.2 fusion.114
  249.6 1.2 fusion.114
  265.8 1.2 fusion.114
  269.0 1.2 fusion.114
  272.2 1.2 fusion.114
  275.5 1.2 fusion.114
  278.7 1.2 fusion.114
  282.0 1.2 fusion.114
  285.2 1.2 fusion.114
  288.4 1.2 fusion.114
  952.9 476.9 %while.29 = (s32[]{:T(128)}, f32[256,256]{1,0:T(8,128)S(1)}, f32[256,256]{1,0:T(8,128)S(1)}, s32[]{:T(128)}, s32[]{:T(128)}) while((s32[]{:T(128)}, f32[256,256]{1,0:T(8,128)S(1)}, f32[256,256]{1,0:T(8,128)S(1)}, s32[]{:T(128)}, s32[]{:T(128)}) %tuple.88), condition=%wide.region_6.0_spmd.clone, body=%wide.region_4.0_spmd.clone.sunk | while | flops 1837314 | bytes 1058916 | solution.py:71
  1429.9 7.0 convolution_convert_fusion
  (3831 shorter events, 1066.7 us)
Async XLA Ops:
  7.2 115.9 %all-reduce.2.cloned.1.call-start = ((), (), s32[]{:S(2)}) async-start(), calls=%async_computation | async-start | bytes 524288 | tf_op jit(solution)/shard_map/psum | solution.py:102
  7.2 10.9 collective-permute-start.1
  7.3 9.8 collective-permute-start
  14.8 3.9 copy-start.1
  26.3 2.5 copy-start
Sparse Core Ops, SparseCore 0:
  31.4 91.6 all-reduce.1
where the time goes:
time: 1470 us; the launch traced here: 1440 us
  other arithmetic  573 us (39%)
  matrix products  547 us (37%)
  loops' own time  201 us (14%)
  waiting for transfers between devices  94.1 us (6%)
    dot_general x256, matrix products, column_step(): jnp.dot(gram, pick, precision=lax.Precision.HIGHEST)  301 us
    another operation x1, loops' own time, upper_factor(): lower = lax.fori_loop(0, order, column_step, jnp.zeros_like(gram))  189 us
    div x256, other arithmetic, row_step(): (pick - jnp.dot(row, solved, precision=lax.Precision.HIGHEST)) / pivot  170 us
    reduce_sum x256, other arithmetic, column_step(): pivot = jnp.sqrt(jnp.sum(column * pick))  170 us
    reduce_sum x256, other arithmetic, row_step(): pivot = jnp.sum(row * pick)  162 us
    psum x1, waiting for transfers between devices, local(): factor = upper_factor(lax.psum(local_gram, 'gx'))  91.8 us
    dot_general x256, matrix products, column_step(): jnp.dot(lower, row, precision=lax.Precision.HIGHEST)  81.5 us
    dot_general x256, matrix products, column_step(): row = jnp.dot(pick, lower, precision=lax.Precision.HIGHEST)  53.6 us
  transfers between devices with their start and end apart: 3, of which 2 were waited for; matrix products, arithmetic and copies ran while one was open for 0% of the time, Pallas kernels for 0%

commit v1 on v0

--- a/solution.py
+++ b/solution.py
@@ -99,8 +99,12 @@
     matrix = sketch.reshape(-1, sketch.shape[-1])
     total = jnp.float32(matrix.shape[0] * lax.axis_size("gx"))
     local_gram = gram_of(matrix) / total
-    factor = upper_factor(lax.psum(local_gram, "gx"))
-    inverse_one = inverse_upper(factor).astype(jnp.bfloat16)
+    gram = lax.psum(local_gram, "gx")
+    lower = lax.linalg.cholesky(gram, symmetrize_input=False)
+    factor = lower.T
+    eye = jnp.eye(gram.shape[0], dtype=gram.dtype)
+    lower_inv = lax.linalg.triangular_solve(lower, eye, left_side=True, lower=True)
+    inverse_one = lower_inv.T.astype(jnp.bfloat16)
     basis = jnp.dot(matrix, inverse_one, preferred_element_type=jnp.float32).astype(jnp.bfloat16)
     return (basis.reshape(sketch.shape), factor)
 

time: 1470 us -> 202 us (0.14); the launches traced: 1440 us -> 201 us
  matrix products: 547 us -> 12.4 us
  other arithmetic: 573 us -> 62.7 us
  loops' own time: 201 us -> 0.03 us
    dot_general x1280 -> x0, matrix products: 537 us -> none  [the longest x256 301 us: column_step(): jnp.dot(gram, pick, precision=lax.Precision.HIGHEST)]
    reduce_sum x512 -> x0, other arithmetic: 332 us -> none  [the longest x256 170 us: column_step(): pivot = jnp.sqrt(jnp.sum(column * pick))]
    another operation x2 -> x1, loops' own time: 201 us -> 0.03 us  [local(): lax.linalg.triangular_solve(lower, eye, left_side=True, lower=True)]
    div x256 -> x0, other arithmetic: 170 us -> none  [row_step(): (pick - jnp.dot(row, solved, precision=lax.Precision.HIGHEST)) / pivot]
    add x768 -> x0, other arithmetic: 59.3 us -> none  [the longest x256 28.7 us: column_step(): return lower + fresh[:, None] * pick[None, :]]
    another operation x0 -> x9, other arithmetic: none -> 54.3 us  [the longest x7 34.6 us: local(): lower = lax.linalg.cholesky(gram, symmetrize_input=False)]
  transfers between devices with their start and end apart: 3 -> 3, of which waited for: 2 -> 2; matrix products, arithmetic and copies ran while one was open for 0% -> 3% of each run, Pallas kernels for 0% -> 0%
where the time goes in v1:
time: 202 us; the launch traced here: 201 us
  waiting for transfers between devices  94 us (47%)
  other arithmetic  62.7 us (31%)
  between operations  15.5 us (8%)
  local copies, waits for them, and re-layouts  13.9 us (7%)
  matrix products  12.4 us (6%)
  starting transfers between devices  2.76 us (1%)
    psum x1, waiting for transfers between devices, local(): gram = lax.psum(local_gram, 'gx')  91.7 us
    another operation x7, other arithmetic, local(): lower = lax.linalg.cholesky(gram, symmetrize_input=False)  34.6 us
    another operation x2, other arithmetic, local(): lax.linalg.triangular_solve(lower, eye, left_side=True, lower=True)  19.7 us
    convert_element_type x1, other arithmetic, local(): sketch = sketch.astype(jnp.bfloat16)  7.55 us
    dot_general x1, matrix products, local(): jnp.dot(matrix, inverse_one, preferred_element_type=jnp.float32)  6.98 us
    unnamed x7, local copies, waits for them, and re-layouts  4.54 us
  transfers between devices with their start and end apart: 3, of which 2 were waited for; matrix products, arithmetic and copies ran while one was open for 3% of the time, Pallas kernels for 0%

profile of v1, /device:TPU:1, one launch (start us, length us, event | category | flops | bytes accessed | tf_op | source)
XLA Modules:
  0.0 201.3 jit_solution(16693057301777906816)
XLA Ops:
  7.2 0.0 all-reduce.3.cloned.1.call-start
  7.2 0.1 collective-permute-start.1
  7.3 2.6 %collective-permute-start = (f32[4,3,3,16,128]{4,3,2,1,0:T(8,128)}, f32[4,3,3,16,128]{4,3,2,1,0:T(8,128)S(1)}, u32[]{:S(2)}, u32[]{:S(2)}) collective-permute-start(f32[4,3,3,16,128]{4,3,2,1,0:T(8,128)} %param.4), channel_id=1, source_target_pairs={{0,1},{1,2},{2,3},{3,4},{4,5},{5,6},{6,7},{7,8},{8,9},{9,10},{10,1... | collective-permute-start | bytes 884744 | tf_op jit(solution)/shard_map/ppermute | solution.py:16
  9.9 1.0 slice_bitcast_fusion.5
  10.9 1.0 slice_bitcast_fusion.4
  11.9 1.0 fusion.64
  13.0 0.2 copy.20
  13.1 0.2 copy.21
  13.3 0.4 fusion.26
  13.6 0.8 fusion.67
  14.5 0.2 copy.24
  14.7 0.2 copy.25
  14.8 0.0 copy-start.1
  14.8 2.3 %collective-permute-done = f32[4,3,3,16,128]{4,3,2,1,0:T(8,128)S(1)} collective-permute-done((f32[4,3,3,16,128]{4,3,2,1,0:T(8,128)}, f32[4,3,3,16,128]{4,3,2,1,0:T(8,128)S(1)}, u32[]{:S(2)}, u32[]{:S(2)}) %collective-permute-start) | collective-permute-done | bytes 294944 | tf_op jit(solution)/shard_map/ppermute | solution.py:16
  17.1 1.0 constant_dynamic-update-slice_fusion.1
  18.1 0.0 collective-permute-done.1
  18.2 0.1 fusion.35
  18.3 0.3 fusion.14
  18.7 0.0 copy-done.1
  18.7 7.5 %add_convert_fusion = bf16[3,3,10,128,256]{4,3,2,1,0:T(8,128)(2,1)S(1)} fusion(bf16[3,3,10,128,256]{4,3,2,1,0:T(8,128)(2,1)S(1)} %copy-done.1, f32[256]{0:T(256)S(1)} %bitcast.90, f32[3,3,10,128]{3,2,1,0:T(8,128)S(1)} %get-tuple-element.27, f32[256]{0:T(256)S(1)} %bitcast.91, f32[3,3,10,128]{3,2,1,0:T(8,128)S(1)} %get-tuple-element.28, f32[256]{0:T(256)S(1)} %bitcast.89, ...), kind=kLoop, calls=%fused_computation.3 | loop fusion | flops 29491200 | bytes 11984896 | tf_op jit(solution)/shard_map/convert_element_type | solution.py:98
  26.3 0.0 copy-start
  26.3 2.5 %copy-done = bf16[3,3,10,128,256]{4,3,2,1,0:T(8,128)(2,1)} copy-done((bf16[3,3,10,128,256]{4,3,2,1,0:T(8,128)(2,1)}, bf16[3,3,10,128,256]{4,3,2,1,0:T(8,128)(2,1)S(1)}, u32[]{:S(2)}) %copy-start) | copy-done | bytes 5898264
  28.8 2.4 %fusion = f32[256,256]{1,0:T(8,128)} fusion(bf16[3,3,10,128,256]{4,3,2,1,0:T(8,128)(2,1)S(1)} %add_convert_fusion), kind=kOutput, calls=%fused_computation.5 | convolution fusion | flops 1510014976 | bytes 6160384 | tf_op jit(solution)/shard_map/dot_general | solution.py:76
  31.2 0.0 all-reduce.3.cloned.1.call-update
  31.3 91.7 %all-reduce.3.cloned.1.call-done = f32[256,256]{1,0:T(8,128)} async-done(((f32[256,256]{1,0:T(8,128)}), f32[256,256]{1,0:T(8,128)}) %all-reduce.3.cloned.1.call-update) | async-done | bytes 262160 | tf_op jit(solution)/shard_map/psum | solution.py:102
  123.0 0.8 cholesky.118
  123.8 11.7 %cholesky.50 = f32[128,128]{1,0:T(8,128)S(1)} custom-call(f32[128,128]{1,0:T(8,128)S(1)} %cholesky.118), custom_call_target="Cholesky" | custom-call | tf_op jit(solution)/shard_map/cholesky | solution.py:103
  135.6 0.6 compare_reduce_fusion.1
  136.2 9.8 %custom-call.11 = f32[1,128,128]{1,2,0:T(8,128)S(1)} custom-call(f32[1,128,128]{2,1,0:T(8,128)S(1)} %get-tuple-element.41), custom_call_target="InvertDiagBlocksLowerTriangular" | custom-call | tf_op jit(solution)/shard_map/cholesky | solution.py:103
  146.1 1.0 constant_dynamic-update-slice_fusion.4
  147.1 1.1 convolution_subtract_fusion.1
  148.2 11.7 %cholesky.105 = f32[128,128]{1,0:T(8,128)S(1)} custom-call(f32[128,128]{1,0:T(8,128)S(1)} %convolution_subtract_fusion.1), custom_call_target="Cholesky" | custom-call | tf_op jit(solution)/shard_map/cholesky | solution.py:103
  160.0 0.7 compare_reduce_fusion
  162.0 1.0 copy.29
  163.0 0.1 triangular_solve.63
  163.0 3.8 %while.1 = (s32[]{:T(128)}, f32[256,256]{1,0:T(8,128)S(1)}, s32[2,2]{1,0:T(2,128)S(1)}, f32[2,128,128]{2,1,0:T(8,128)S(1)}, s32[]{:T(128)}) while((s32[]{:T(128)}, f32[256,256]{1,0:T(8,128)S(1)}, s32[2,2]{1,0:T(2,128)S(1)}, f32[2,128,128]{2,1,0:T(8,128)S(1)}, s32[]{:T(128)}) %tuple.43), condition=%wide.while_cond, body=%wide.while_body.sunk | while | flops 2 | bytes 131189 | solution.py:106
  163.0 0.6 fusion.77
  163.7 1.3 bitcast_dynamic-update-slice_fusion.2
  165.0 0.6 fusion.77
  165.6 1.3 bitcast_dynamic-update-slice_fusion.2
  166.9 19.7 %custom-call.12 = f32[2,128,128]{1,2,0:T(8,128)S(1)} custom-call(f32[2,128,128]{2,1,0:T(8,128)S(1)} %get-tuple-element.9), custom_call_target="InvertDiagBlocksLowerTriangular" | custom-call | tf_op jit(solution)/shard_map/triangular_solve | solution.py:106
  186.6 0.3 fusion.68
  186.8 0.3 convolution_subtract_fusion
  187.1 0.3 convolution_convert_fusion.1
  187.4 7.0 %convolution_convert_fusion = bf16[11520,256]{1,0:T(8,128)(2,1)} fusion(bf16[11520,256]{1,0:T(8,128)(2,1)} %bitcast.86, bf16[128,256]{1,0:T(8,128)(2,1)S(1)} %convolution_convert_fusion.1, bf16[128,256]{1,0:T(8,128)(2,1)S(1)} %get-tuple-element.52), kind=kOutput, calls=%fused_computation.2 | convolution fusion | flops 1513160704 | bytes 11927552 | tf_op jit(solution)/shard_map/dot_general | solution.py:108
  (17 shorter events, 0.3 us)
Async XLA Ops:
  7.2 115.8 %all-reduce.3.cloned.1.call-start = ((), (), s32[]{:S(2)}) async-start(), calls=%async_computation | async-start | bytes 524288 | tf_op jit(solution)/shard_map/psum | solution.py:102
  7.2 10.9 %collective-permute-start.1 = (f32[4,3,3,16,128]{4,3,2,1,0:T(8,128)}, f32[4,3,3,16,128]{4,3,2,1,0:T(8,128)S(1)}, u32[]{:S(2)}, u32[]{:S(2)}) collective-permute-start(f32[4,3,3,16,128]{4,3,2,1,0:T(8,128)} %param.4), channel_id=1, source_target_pairs={{1,0},{2,1},{3,2},{4,3},{5,4},{6,5},{7,6},{8,7},{9,8},{10,9},{11,1... | collective-permute-start | bytes 884744 | tf_op jit(solution)/shard_map/ppermute | solution.py:18
  7.3 9.8 %collective-permute-start = (f32[4,3,3,16,128]{4,3,2,1,0:T(8,128)}, f32[4,3,3,16,128]{4,3,2,1,0:T(8,128)S(1)}, u32[]{:S(2)}, u32[]{:S(2)}) collective-permute-start(f32[4,3,3,16,128]{4,3,2,1,0:T(8,128)} %param.4), channel_id=1, source_target_pairs={{0,1},{1,2},{2,3},{3,4},{4,5},{5,6},{6,7},{7,8},{8,9},{9,10},{10,1... | collective-permute-start | bytes 884744 | tf_op jit(solution)/shard_map/ppermute | solution.py:16
  14.8 3.9 %copy-start.1 = (bf16[3,3,10,128,256]{4,3,2,1,0:T(8,128)(2,1)S(1)}, bf16[3,3,10,128,256]{4,3,2,1,0:T(8,128)(2,1)}, u32[]{:S(2)}) copy-start(bf16[3,3,10,128,256]{4,3,2,1,0:T(8,128)(2,1)} %param.6) | copy-start | bytes 17694724
  26.3 2.5 %copy-start = (bf16[3,3,10,128,256]{4,3,2,1,0:T(8,128)(2,1)}, bf16[3,3,10,128,256]{4,3,2,1,0:T(8,128)(2,1)S(1)}, u32[]{:S(2)}) copy-start(bf16[3,3,10,128,256]{4,3,2,1,0:T(8,128)(2,1)S(1)} %add_convert_fusion) | copy-start | bytes 17694724
Sparse Core Ops, SparseCore 0:
  31.4 91.5 all-reduce.2
